TPU v7x, 32 devices: a whole 2x2x4 slice. The times are simulated.
32 devices in a mesh: grp: 4 (over y, core), shard: 8 (over z, x).
Axes of the slice: x: 2, y: 2, z: 4, core: 2. Of those that a mesh axis runs over, the one named last changes fastest.
Arguments:
- query_rows: bfloat16 [16, 6144], P('grp'), may hold values from -10 to 10
- key_cache: bfloat16 [16, 2048, 1024], P('grp', 'shard'), may hold values from -10 to 10
- value_cache: bfloat16 [16, 2048, 1024], P('grp', 'shard'), may hold values from -6 to 6
- lengths: int32 [16], P('grp'), may hold values from 2 to 2048
- attn_gain: float32 [6144], replicated, may hold values from 0.5 to 1.5
- router: bfloat16 [6144, 4], replicated, may hold values from -0.078125 to 0.078125
- expert_ids: int32 [16, 2], replicated, may hold values from 0 to 3, all different within a row; in each aligned block of 4 rows (0 to 3, 4 to 7, ...) at most 2 rows name the same one
- w_gate: bfloat16 [4, 6144, 8192], P('grp', None, 'shard'), may hold values from -0.078125 to 0.078125
- w_up: bfloat16 [4, 6144, 8192], P('grp', None, 'shard'), may hold values from -0.078125 to 0.078125
- w_down: bfloat16 [4, 8192, 6144], P('grp', 'shard'), may hold values from -0.0625 to 0.0625
Outputs:
- normed: bfloat16 [16, 6144], P('grp')
- expert_out: bfloat16 [16, 6144], P('grp', 'shard')
Inputs may be any that keep to these rules, and one draw needn't show every extreme that they name: `expert_ids`: the two ids of a row differ. Among the 4 rows of one index of grp (aligned blocks), no expert is named by more than 2 rows, a bound that some block reaches.
All inputs are finite; a program needn't handle non-finite values.
Results may differ from a plain program's by a relative error of at most 0.0095.
Values may be sent and summed in bfloat16 or wider, within the bound.
No kernel may reach another device: no remote copies, remote signals or barrier semaphores. Data moves between devices by JAX's collectives and lax.ppermute only.
A program may use at most 128 MiB of HBM per device.

v0:
```python
import math
import jax
import jax.numpy as jnp
from jax import lax
from jax.sharding import PartitionSpec as P

HEADS = 48
KV_HEADS = 8
HEAD_DIM = 128
NEG_FILL = -1e30


def combined_all(value, axis, join):
    pieces = jax.tree.map(lambda part: lax.all_gather(part, axis), value)
    head = jax.tree.map(lambda part: part[0], pieces)
    tail = jax.tree.map(lambda part: part[1:], pieces)
    total, _ = lax.scan(lambda total, share: (join(total, share), None), head, tail)
    return total


def merge_parts(earlier, second):
    joint_max = jnp.maximum(earlier[0], second[0])
    left_scale = jnp.exp(earlier[0] - joint_max)
    right_scale = jnp.exp(second[0] - joint_max)
    joint_sum = earlier[1] * left_scale + second[1] * right_scale
    joint_mix = earlier[2] * left_scale[..., None] + second[2] * right_scale[..., None]
    return (joint_max, joint_sum, joint_mix)


def shards(
    query_rows, key_cache, value_cache, lengths, attn_gain, router, expert_ids, w_gate, w_up, w_down
):
    rows_here = query_rows.shape[0]
    span = key_cache.shape[1]
    kv_share = HEADS // KV_HEADS
    shard_id = lax.axis_index("shard")
    query_heads = query_rows.reshape(rows_here, KV_HEADS, kv_share, HEAD_DIM)
    key_heads = key_cache.reshape(rows_here, span, KV_HEADS, HEAD_DIM)
    value_heads = value_cache.reshape(rows_here, span, KV_HEADS, HEAD_DIM)
    scores = jnp.einsum(
        "rgjd,rtgd->rgjt", query_heads, key_heads, preferred_element_type=jnp.float32
    ) / math.sqrt(HEAD_DIM)
    position = shard_id * span + jnp.arange(span, dtype=jnp.int32)
    live_mask = (position[None, :] < lengths[:, None])[:, None, None, :]
    scores = jnp.where(live_mask, scores, NEG_FILL)
    block_max = jnp.max(scores, axis=-1)
    block_probs = jnp.where(live_mask, jnp.exp(scores - block_max[..., None]), 0.0).astype(
        jnp.bfloat16
    )
    block_sum = jnp.sum(block_probs.astype(jnp.float32), axis=-1)
    block_mix = jnp.einsum(
        "rgjt,rtgd->rgjd", block_probs, value_heads, preferred_element_type=jnp.float32
    )
    whole_max, whole_sum, whole_mix = combined_all(
        (block_max, block_sum, block_mix), "shard", merge_parts
    )
    attended = (whole_mix / whole_sum[..., None]).reshape(rows_here, -1)
    mean_square = jnp.mean(attended * attended, axis=-1, keepdims=True)
    normed = (attended * lax.rsqrt(mean_square + 1e-05) * attn_gain).astype(jnp.bfloat16)
    experts = router.shape[1]
    capacity = rows_here // 2
    width = normed.shape[1]
    logits = jnp.dot(normed, router, preferred_element_type=jnp.float32)
    own_ids = lax.dynamic_slice_in_dim(expert_ids, lax.axis_index("grp") * rows_here, rows_here, 0)
    expert_range = jnp.arange(experts, dtype=jnp.int32)
    expert_hit = own_ids[:, :, None] == expert_range[None, None, :]
    chosen = jnp.sum(jnp.where(expert_hit, logits[:, None, :], 0.0), axis=-1)
    first_weight = jax.nn.sigmoid(chosen[:, 0] - chosen[:, 1])
    route_weight = jnp.stack([first_weight, 1.0 - first_weight], axis=1)
    row_range = jnp.arange(rows_here, dtype=jnp.int32)
    strictly_lower = (row_range[:, None] > row_range[None, :]).astype(jnp.float32)
    counts = jnp.sum(expert_hit, axis=1).astype(jnp.float32)
    before = jnp.dot(
        strictly_lower, counts, precision=lax.Precision.HIGHEST, preferred_element_type=jnp.float32
    )
    slot_index = jnp.sum(jnp.where(expert_hit, before[:, None, :], 0.0), axis=-1)
    slot_base = jnp.sum(
        jnp.where(expert_hit, (expert_range * capacity).astype(jnp.float32)[None, None, :], 0.0),
        axis=-1,
    )
    destination = slot_base + slot_index
    slot_columns = jnp.arange(experts * capacity, dtype=jnp.int32).astype(jnp.float32)
    placed = (destination[:, :, None] == slot_columns[None, None, :]).astype(jnp.float32)
    send_matrix = jnp.sum(placed, axis=1)
    combine_matrix = jnp.sum(placed * route_weight[:, :, None], axis=1)
    gate_local = w_gate[0]
    up_local = w_up[0]
    down_local = w_down[0]
    outgoing = jnp.einsum(
        "rc,rd->cd", send_matrix.astype(jnp.bfloat16), normed, preferred_element_type=jnp.float32
    )
    outgoing = outgoing.astype(jnp.bfloat16).reshape(experts, capacity, width)
    arrived = lax.all_to_all(outgoing, "grp", split_axis=0, concat_axis=0, tiled=True)
    gate_proj = jnp.einsum("gcd,df->gcf", arrived, gate_local, preferred_element_type=jnp.float32)
    up_proj = jnp.einsum("gcd,df->gcf", arrived, up_local, preferred_element_type=jnp.float32)
    hidden = (jax.nn.silu(gate_proj) * up_proj).astype(jnp.bfloat16)
    partial_value = jnp.einsum(
        "gcf,fd->gcd", hidden, down_local, preferred_element_type=jnp.float32
    )
    summed = lax.psum(partial_value, "shard")
    returned = lax.all_to_all(summed, "grp", split_axis=0, concat_axis=0, tiled=True)
    full_rows = jnp.dot(
        combine_matrix,
        returned.reshape(experts * capacity, width),
        precision=lax.Precision.HIGHEST,
        preferred_element_type=jnp.float32,
    )
    out_width = width // lax.axis_size("shard")
    result = lax.dynamic_slice_in_dim(full_rows, shard_id * out_width, out_width, 1)
    return (normed, result.astype(jnp.bfloat16))


def solution(mesh):
    in_specs = (
        P("grp", None),
        P("grp", "shard", None),
        P("grp", "shard", None),
        P("grp"),
        P(),
        P(),
        P(),
        P("grp", None, "shard"),
        P("grp", None, "shard"),
        P("grp", "shard", None),
    )
    out_specs = (P("grp", None), P("grp", "shard"))
    return jax.shard_map(shards, mesh=mesh, in_specs=in_specs, out_specs=out_specs, check_vma=False)
```

profile of v0, /device:TPU:0, one launch (start us, length us, event | category | flops | bytes accessed | tf_op | source)
XLA Modules:
  0.0 222.4 jit_solution(8904298598831475986)
XLA Ops:
  7.2 0.0 copy-start
  7.2 0.0 all-reduce.2.cloned.1.call-start
  7.3 1.0 reshape.80
  8.3 0.9 broadcast_compare_fusion
  9.2 0.7 fusion.36
  9.9 32.4 %all-gather = f32[32,8,6]{2,1,0:T(8,128)S(1)} all-gather(f32[4,8,6]{2,1,0:T(8,128)S(1)} %get-tuple-element.90), channel_id=2, replica_groups=mesh['grp'=4,'shard'=8] {'shard'}, dimensions={0}, use_global_device_ids=true | all-gather | bytes 6912 | tf_op jit(solution)/shard_map/all_gather | solution.py:14
  42.3 0.2 convert_reduce_fusion
  42.5 30.5 %all-gather.1 = f32[32,8,6]{2,1,0:T(8,128)S(1)} all-gather(f32[4,8,6]{2,1,0:T(8,128)S(1)} %convert_reduce_fusion), channel_id=3, replica_groups=mesh['grp'=4,'shard'=8] {'shard'}, dimensions={0}, use_global_device_ids=true | all-gather | bytes 6912 | tf_op jit(solution)/shard_map/all_gather | solution.py:14
  73.0 0.0 copy-start.4
  73.1 0.4 fusion.10
  73.5 31.6 %all-gather.2 = f32[32,8,6,128]{3,1,2,0:T(8,128)S(1)} all-gather(f32[4,8,6,128]{3,1,2,0:T(8,128)S(1)} %copy.53), channel_id=4, replica_groups=mesh['grp'=4,'shard'=8] {'shard'}, dimensions={0}, use_global_device_ids=true | all-gather | bytes 884736 | tf_op jit(solution)/shard_map/all_gather | solution.py:14
  105.2 0.1 constant_dynamic-slice_fusion.1
  105.3 0.1 convert_reduce_fusion.1
  105.4 0.1 fusion.31
  105.5 0.1 copy.56
  105.6 0.2 copy.59
  105.8 0.1 copy.57
  105.9 0.2 copy.60
  106.2 0.1 copy.58
  106.3 0.0 copy-start.3
  106.3 3.0 %while.14 = (s32[]{:T(128)}, f32[4,8,6]{1,0,2:T(4,128)S(1)}, f32[4,8,6]{1,0,2:T(4,128)S(1)}, f32[4,8,6,128]{3,2,1,0:T(8,128)S(1)}, f32[7,4,8,6]{2,1,3,0:T(4,128)...) while((s32[]{:T(128)}, f32[4,8,6]{1,0,2:T(4,128)S(1)}, ...), condition=%wide.region_3.4_spmd, body=%wide.region_2.3_spmd.sunk | while | flops 74882 | bytes 502373 | solution.py:17
  106.3 0.1 copy.97
  106.4 0.1 copy.98
  106.5 0.2 fusion.53
  106.7 0.1 copy.97
  106.8 0.1 copy.98
  107.0 0.2 fusion.53
  107.2 0.1 copy.97
  107.3 0.1 copy.98
  107.4 0.2 fusion.53
  107.6 0.1 copy.97
  107.7 0.1 copy.98
  107.8 0.2 fusion.53
  108.0 0.1 copy.97
  108.1 0.1 copy.98
  108.2 0.2 fusion.53
  108.4 0.1 copy.97
  108.5 0.1 copy.98
  108.6 0.2 fusion.53
  108.9 0.1 copy.97
  109.0 0.1 copy.98
  109.1 0.2 fusion.53
  109.2 0.1 copy.62
  109.3 0.2 multiply_reduce_fusion
  109.6 0.1 multiply_convert_fusion
  109.7 0.0 copy-start.2
  109.7 0.2 fusion.37
  109.9 0.2 select_reduce_fusion.1
  110.1 0.1 fusion.30
  110.2 0.2 convolution_convert_fusion
  110.4 0.1 reshape.84
  110.5 6.9 %all_to_all.10 = bf16[4,2,6144]{2,1,0:T(2,128)(2,1)S(1)} all-to-all(bf16[4,2,6144]{2,1,0:T(2,128)(2,1)S(1)} %reshape.84), channel_id=1, replica_groups=mesh['grp'=4,'shard'=8] {'grp'}, dimensions={0} | all-to-all | bytes 196608 | tf_op jit(solution)/shard_map/all_to_all | solution.py:93
  117.4 6.8 %fusion.8 = f32[4,2,1024]{2,1,0:T(2,128)S(1)} fusion(bf16[4,2,6144]{2,1,0:T(2,128)(2,1)S(1)} %all_to_all.10, bf16[1,6144,1024]{2,1,0:T(8,128)(2,1)} %param.19), kind=kOutput, calls=%fused_computation.14 | convolution fusion | flops 100663296 | bytes 12713984 | tf_op jit(solution)/shard_map/gcd,df->gcf/dot_general | solution.py:94
  124.2 0.0 slice-start.2
  124.2 6.7 %fusion.25 = bf16[4,2,1024]{2,1,0:T(2,128)(2,1)S(1)} fusion(bf16[4,2,6144]{2,1,0:T(2,128)(2,1)S(1)} %all_to_all.10, bf16[1,6144,1024]{2,1,0:T(8,128)(2,1)} %param.20, f32[4,2,1024]{2,1,0:T(2,128)S(1)} %fusion.8), kind=kOutput, calls=%fused_computation.26 | convolution fusion | flops 100712448 | bytes 12730368 | tf_op jit(solution)/shard_map/gcd,df->gcf/dot_general | solution.py:95
  130.9 2.5 %fusion.4 = f32[4,2,6144]{2,0,1:T(4,128)} fusion(bf16[1,1024,6144]{2,1,0:T(8,128)(2,1)S(1)} %bitcast.70, bf16[4,2,1024]{2,1,0:T(2,128)(2,1)S(1)} %fusion.25), kind=kOutput, calls=%fused_computation.10 | convolution fusion | flops 100663296 | bytes 12795904 | tf_op jit(solution)/shard_map/gcf,fd->gcd/dot_general | solution.py:97
  133.4 0.0 all-reduce.2.cloned.1.call-update
  133.5 70.6 %all-reduce.2.cloned.1.call-done = f32[4,2,6144]{2,0,1:T(4,128)} async-done(((f32[4,2,6144]{2,0,1:T(4,128)}), f32[4,2,6144]{2,0,1:T(4,128)}) %all-reduce.2.cloned.1.call-update) | async-done | bytes 196624 | tf_op jit(solution)/shard_map/psum | solution.py:100
  204.1 1.8 copy.64
  205.8 3.4 %all-to-all-start.1 = ((f32[4,2,6144]{2,1,0:T(2,128)}), f32[4,2,6144]{2,1,0:T(2,128)S(1)}, u32[]{:S(2)}, u32[]{:S(2)}) async-start(f32[4,2,6144]{2,1,0:T(2,128)} %copy.64), calls=%async_computation.1 | async-start | bytes 393216 | tf_op jit(solution)/shard_map/all_to_all | solution.py:101
  209.2 5.3 %all-to-all-done.1 = f32[4,2,6144]{2,1,0:T(2,128)S(1)} async-done(((f32[4,2,6144]{2,1,0:T(2,128)}), f32[4,2,6144]{2,1,0:T(2,128)S(1)}, u32[]{:S(2)}, u32[]{:S(2)}) %all-to-all-start.1) | async-done | bytes 196640 | tf_op jit(solution)/shard_map/all_to_all | solution.py:101
  214.5 0.1 reshape.85
  214.6 0.3 fusion.38
  214.9 0.6 dynamic-slice_convert_fusion
  (43 shorter events, 0.5 us)
Async XLA Ops:
  7.2 2.0 copy-start
  7.2 196.9 %all-reduce.2.cloned.1.call-start = ((), (), s32[]{:S(2)}) async-start(), calls=%async_computation.2 | async-start | bytes 393216 | tf_op jit(solution)/shard_map/psum | solution.py:100
  8.3 64.8 %copy-start.1 = (bf16[4,256,1024]{2,1,0:T(8,128)(2,1)S(1)}, bf16[4,256,1024]{2,1,0:T(8,128)(2,1)}, u32[]{:S(2)}) copy-start(bf16[4,256,1024]{2,1,0:T(8,128)(2,1)} %param.14) | copy-start | bytes 6291460
  73.0 32.2 %copy-start.4 = (s32[16,2]{0,1:T(2,128)S(1)}, s32[16,2]{0,1:T(2,128)}, u32[]{:S(2)}) copy-start(s32[16,2]{0,1:T(2,128)} %param.18) | copy-start | bytes 388
  106.3 3.4 %copy-start.3 = (f32[6144]{0:T(1024)S(1)}, f32[6144]{0:T(1024)}, u32[]{:S(2)}) copy-start(f32[6144]{0:T(1024)} %param.16) | copy-start | bytes 73732
  106.3 3.5 %copy-start.5 = (bf16[6144,4]{0,1:T(4,128)(2,1)S(1)}, bf16[6144,4]{0,1:T(4,128)(2,1)}, u32[]{:S(2)}) copy-start(bf16[6144,4]{0,1:T(4,128)(2,1)} %param.17) | copy-start | bytes 147460
  109.7 14.4 %copy-start.2 = (bf16[4,6144]{1,0:T(4,128)(2,1)}, bf16[4,6144]{1,0:T(4,128)(2,1)S(1)}, u32[]{:S(2)}) copy-start(bf16[4,6144]{1,0:T(4,128)(2,1)S(1)} %multiply_convert_fusion) | copy-start | bytes 147460
  117.4 13.5 %slice-start = ((s8[12582912]{0:T(1024)(128)(4,1)}), s8[4194304]{0:T(1024)(128)(4,1)S(1)}, s32[]{:S(2)}) async-start(s8[12582912]{0:T(1024)(128)(4,1)} %bitcast.69), calls=%async_computation.3 | async-start | bytes 8388608
  117.4 13.5 %slice-start.1 = ((s8[12582912]{0:T(1024)(128)(4,1)}), s8[4194304]{0:T(1024)(128)(4,1)S(1)}, s32[]{:S(2)}) async-start(s8[12582912]{0:T(1024)(128)(4,1)} %bitcast.69), calls=%async_computation.4 | async-start | bytes 8388608
  124.2 6.7 %slice-start.2 = ((s8[12582912]{0:T(1024)(128)(4,1)}), s8[4194304]{0:T(1024)(128)(4,1)S(1)}, s32[]{:S(2)}) async-start(s8[12582912]{0:T(1024)(128)(4,1)} %bitcast.69), calls=%async_computation.5 | async-start | bytes 8388608
  205.8 8.7 %all-to-all-start.1 = ((f32[4,2,6144]{2,1,0:T(2,128)}), f32[4,2,6144]{2,1,0:T(2,128)S(1)}, u32[]{:S(2)}, u32[]{:S(2)}) async-start(f32[4,2,6144]{2,1,0:T(2,128)} %copy.64), calls=%async_computation.1 | async-start | bytes 393216 | tf_op jit(solution)/shard_map/all_to_all | solution.py:101
Sparse Core Ops, SparseCore 0:
  133.6 70.4 all-reduce.1
where the time goes:
time: 223 us; the launch traced here: 222 us
  blocking collectives  101 us (45%)
  waiting for transfers between devices  75.9 us (34%)
  matrix products  17.9 us (8%)
  between operations  14.3 us (6%)
  local copies, waits for them, and re-layouts  6.13 us (3%)
  starting transfers between devices  3.4 us (2%)
  other arithmetic  3.13 us (1%)
    all_gather x3, blocking collectives, combined_all(): pieces = jax.tree.map(lambda part: lax.all_gather(part, axis), value)  94.5 us
    psum x1, waiting for transfers between devices, shards(): summed = lax.psum(partial_value, 'shard')  70.6 us
    all_to_all x1, blocking collectives, shards(): lax.all_to_all(outgoing, 'grp', split_axis=0, concat_axis=0, tiled=True)  6.89 us
    dot_general x1, matrix products, shards(): jnp.einsum('gcd,df->gcf', arrived, gate_local, preferred_element_type=jnp...  6.76 us
    dot_general x1, matrix products, shards(): jnp.einsum('gcd,df->gcf', arrived, up_local, preferred_element_type=jnp.f...  6.69 us
    all_to_all x1, waiting for transfers between devices, shards(): lax.all_to_all(summed, 'grp', split_axis=0, concat_axis=0, tiled=True)  5.29 us
  transfers between devices with their start and end apart: 2, of which 2 were waited for; matrix products, arithmetic and copies ran while one was open for 0% of the time, Pallas kernels for 0%

commit v1 on v0

--- a/solution.py
+++ b/solution.py
@@ -97,7 +97,7 @@
     partial_value = jnp.einsum(
         "gcf,fd->gcd", hidden, down_local, preferred_element_type=jnp.float32
     )
-    summed = lax.psum(partial_value, "shard")
+    summed = jnp.sum(lax.all_gather(partial_value, "shard"), axis=0)
     returned = lax.all_to_all(summed, "grp", split_axis=0, concat_axis=0, tiled=True)
     full_rows = jnp.dot(
         combine_matrix,

time: 223 us -> 201 us (0.901)
  waiting for transfers between devices: 75.9 us -> 50.1 us
  matrix products: 17.9 us -> 21 us
  other arithmetic: 3.13 us -> 5.89 us
    psum x1 -> x0, waiting for transfers between devices: 70.6 us -> none  [shards(): summed = lax.psum(partial_value, 'shard')]
    all_gather x0 -> x1, waiting for transfers between devices: none -> 44.8 us  [shards(): summed = jnp.sum(lax.all_gather(partial_value, 'shard'), axis=0)]
    dot_general x1, matrix products: 2.5 us -> 12.5 us  [shards(): jnp.einsum('gcf,fd->gcd', hidden, down_local, preferred_element_type=jnp....]
    dot_general x1 -> x0, matrix products: 6.69 us -> none  [shards(): jnp.einsum('gcd,df->gcf', arrived, up_local, preferred_element_type=jnp.f...]
    reduce_sum x0 -> x1, other arithmetic: none -> 2.76 us  [shards(): summed = jnp.sum(lax.all_gather(partial_value, 'shard'), axis=0)]
where the time goes in v1:
time: 201 us
  blocking collectives  101 us (50%)
  waiting for transfers between devices  50.1 us (25%)
  matrix products  21 us (10%)
  between operations  14.3 us (7%)
  other arithmetic  5.89 us (3%)
  local copies, waits for them, and re-layouts  4.35 us (2%)
  starting transfers between devices  3.4 us (2%)
    all_gather x3, blocking collectives, combined_all(): pieces = jax.tree.map(lambda part: lax.all_gather(part, axis), value)  94.5 us
    all_gather x1, waiting for transfers between devices, shards(): summed = jnp.sum(lax.all_gather(partial_value, 'shard'), axis=0)  44.8 us
    dot_general x1, matrix products, shards(): jnp.einsum('gcf,fd->gcd', hidden, down_local, preferred_element_type=jnp....  12.5 us
    all_to_all x1, blocking collectives, shards(): lax.all_to_all(outgoing, 'grp', split_axis=0, concat_axis=0, tiled=True)  6.89 us
    dot_general x1, matrix products, shards(): jnp.einsum('gcd,df->gcf', arrived, gate_local, preferred_element_type=jnp...  6.53 us
    all_to_all x1, waiting for transfers between devices, shards(): lax.all_to_all(summed, 'grp', split_axis=0, concat_axis=0, tiled=True)  5.29 us
  transfers between devices with their start and end apart: 2, of which 2 were waited for; matrix products, arithmetic and copies ran while one was open for 0% of the time, Pallas kernels for 0%

profile of v1, /device:TPU:0, one launch (start us, length us, event | category | flops | bytes accessed | tf_op | source)
XLA Modules:
  0.0 200.7 jit_solution(14880913598832021265)
XLA Ops:
  7.2 0.0 copy-start
  7.2 0.0 all-gather.6.cloned.1.call-start
  7.3 1.0 reshape.80
  8.3 0.0 copy-start.1
  8.3 0.9 broadcast_compare_fusion
  9.2 0.7 fusion.42
  9.9 32.4 %all-gather = f32[32,8,6]{2,1,0:T(8,128)S(1)} all-gather(f32[4,8,6]{2,1,0:T(8,128)S(1)} %get-tuple-element.104), channel_id=2, replica_groups=mesh['grp'=4,'shard'=8] {'shard'}, dimensions={0}, use_global_device_ids=true | all-gather | bytes 6912 | tf_op jit(solution)/shard_map/all_gather | solution.py:14
  42.3 0.2 convert_reduce_fusion
  42.5 30.5 %all-gather.1 = f32[32,8,6]{2,1,0:T(8,128)S(1)} all-gather(f32[4,8,6]{2,1,0:T(8,128)S(1)} %convert_reduce_fusion), channel_id=3, replica_groups=mesh['grp'=4,'shard'=8] {'shard'}, dimensions={0}, use_global_device_ids=true | all-gather | bytes 6912 | tf_op jit(solution)/shard_map/all_gather | solution.py:14
  73.0 0.0 copy-start.4
  73.1 0.4 fusion.10
  73.5 31.6 %all-gather.2 = f32[32,8,6,128]{3,1,2,0:T(8,128)S(1)} all-gather(f32[4,8,6,128]{3,1,2,0:T(8,128)S(1)} %copy.91), channel_id=4, replica_groups=mesh['grp'=4,'shard'=8] {'shard'}, dimensions={0}, use_global_device_ids=true | all-gather | bytes 884736 | tf_op jit(solution)/shard_map/all_gather | solution.py:14
  105.2 0.1 constant_dynamic-slice_fusion.1
  105.3 0.1 convert_reduce_fusion.1
  105.4 0.1 fusion.36
  105.5 0.1 copy.94
  105.6 0.2 copy.97
  105.9 0.1 copy.95
  106.0 0.2 copy.98
  106.2 0.1 copy.96
  106.3 0.0 copy-start.3
  106.3 0.0 copy-start.5
  106.3 3.0 %while.14 = (s32[]{:T(128)}, f32[4,8,6]{1,0,2:T(4,128)S(1)}, f32[4,8,6]{1,0,2:T(4,128)S(1)}, f32[4,8,6,128]{3,2,1,0:T(8,128)S(1)}, f32[7,4,8,6]{2,1,3,0:T(4,128)...) while((s32[]{:T(128)}, f32[4,8,6]{1,0,2:T(4,128)S(1)}, ...), condition=%wide.region_3.4_spmd, body=%wide.region_2.3_spmd.sunk | while | flops 74882 | bytes 502373 | solution.py:17
  106.3 0.1 copy.138
  106.4 0.1 copy.139
  106.5 0.2 fusion.59
  106.8 0.1 copy.138
  106.9 0.1 copy.139
  107.0 0.2 fusion.59
  107.2 0.1 copy.138
  107.3 0.1 copy.139
  107.4 0.2 fusion.59
  107.6 0.1 copy.138
  107.7 0.1 copy.139
  107.8 0.2 fusion.59
  108.0 0.1 copy.138
  108.1 0.1 copy.139
  108.2 0.2 fusion.59
  108.5 0.1 copy.138
  108.6 0.1 copy.139
  108.7 0.2 fusion.59
  108.9 0.1 copy.138
  109.0 0.1 copy.139
  109.1 0.2 fusion.59
  109.3 0.1 copy.100
  109.4 0.2 multiply_reduce_fusion
  109.6 0.1 multiply_convert_fusion
  109.7 0.0 copy-start.2
  109.8 0.2 fusion.43
  109.9 0.2 select_reduce_fusion.1
  110.1 0.1 fusion.35
  110.2 0.2 convolution_convert_fusion
  110.4 0.1 reshape.84
  110.5 6.9 %all_to_all.10 = bf16[4,2,6144]{2,1,0:T(2,128)(2,1)S(1)} all-to-all(bf16[4,2,6144]{2,1,0:T(2,128)(2,1)S(1)} %reshape.84), channel_id=1, replica_groups=mesh['grp'=4,'shard'=8] {'grp'}, dimensions={0} | all-to-all | bytes 196608 | tf_op jit(solution)/shard_map/all_to_all | solution.py:93
  117.4 6.5 %fusion.8 = f32[4,2,1024]{2,1,0:T(2,128)S(1)} fusion(bf16[4,2,6144]{2,1,0:T(2,128)(2,1)S(1)} %all_to_all.10, bf16[1,6144,1024]{2,1,0:T(8,128)(2,1)} %param.19), kind=kOutput, calls=%fused_computation.14 | convolution fusion | flops 100663296 | bytes 12713984 | tf_op jit(solution)/shard_map/gcd,df->gcf/dot_general | solution.py:94
  124.0 12.5 %fusion.4 = f32[4,2,6144]{2,1,0:T(2,128)} fusion(bf16[1,1024,6144]{2,1,0:T(8,128)(2,1)} %param.21, bf16[4,2,6144]{2,1,0:T(2,128)(2,1)S(1)} %all_to_all.10, bf16[1,6144,1024]{2,1,0:T(8,128)(2,1)} %param.20, f32[4,2,1024]{2,1,0:T(2,128)S(1)} %fusion.8), kind=kOutput, calls=%fused_computation.10 | convolution fusion | flops 201375744 | bytes 25493504 | tf_op jit(solution)/shard_map/gcf,fd->gcd/dot_general | solution.py:97
  136.5 0.0 all-gather.6.cloned.1.call-update
  136.5 44.8 %all-gather.6.cloned.1.call-done = f32[32,2,6144]{2,1,0:T(2,128)} async-done(((f32[4,2,6144]{2,1,0:T(2,128)}), f32[32,2,6144]{2,1,0:T(2,128)}) %all-gather.6.cloned.1.call-update) | async-done | bytes 1572880 | tf_op jit(solution)/shard_map/all_gather | solution.py:100
  181.3 2.8 %reduce_sum.89 = f32[4,2,6144]{2,1,0:T(2,128)} reduce(f32[8,4,2,6144]{3,2,1,0:T(2,128)} %bitcast.73, f32[]{:T(128)} %constant.17.clone.1), dimensions={0}, to_apply=%region_11.12 | reduce | flops 344064 | bytes 1769476 | tf_op jit(solution)/shard_map/reduce_sum | solution.py:100
  184.1 3.4 %all-to-all-start.1 = ((f32[4,2,6144]{2,1,0:T(2,128)}), f32[4,2,6144]{2,1,0:T(2,128)S(1)}, u32[]{:S(2)}, u32[]{:S(2)}) async-start(f32[4,2,6144]{2,1,0:T(2,128)} %reduce_sum.89), calls=%async_computation.1 | async-start | bytes 393216 | tf_op jit(solution)/shard_map/all_to_all | solution.py:101
  187.5 5.3 %all-to-all-done.1 = f32[4,2,6144]{2,1,0:T(2,128)S(1)} async-done(((f32[4,2,6144]{2,1,0:T(2,128)}), f32[4,2,6144]{2,1,0:T(2,128)S(1)}, u32[]{:S(2)}, u32[]{:S(2)}) %all-to-all-start.1) | async-done | bytes 196640 | tf_op jit(solution)/shard_map/all_to_all | solution.py:101
  192.8 0.1 reshape.85
  192.9 0.3 fusion.44
  193.2 0.6 dynamic-slice_convert_fusion
  (35 shorter events, 0.5 us)
Async XLA Ops:
  7.2 2.0 copy-start
  7.2 174.2 %all-gather.6.cloned.1.call-start = ((), (), s32[]{:S(2)}) async-start(), calls=%async_computation.2 | async-start | bytes 1769472 | tf_op jit(solution)/shard_map/all_gather | solution.py:100
  8.3 64.8 %copy-start.1 = (bf16[4,256,1024]{2,1,0:T(8,128)(2,1)S(1)}, bf16[4,256,1024]{2,1,0:T(8,128)(2,1)}, u32[]{:S(2)}) copy-start(bf16[4,256,1024]{2,1,0:T(8,128)(2,1)} %param.14) | copy-start | bytes 6291460
  73.0 32.2 %copy-start.4 = (s32[16,2]{0,1:T(2,128)S(1)}, s32[16,2]{0,1:T(2,128)}, u32[]{:S(2)}) copy-start(s32[16,2]{0,1:T(2,128)} %param.18) | copy-start | bytes 388
  106.3 3.4 %copy-start.3 = (f32[6144]{0:T(1024)S(1)}, f32[6144]{0:T(1024)}, u32[]{:S(2)}) copy-start(f32[6144]{0:T(1024)} %param.16) | copy-start | bytes 73732
  106.3 3.5 %copy-start.5 = (bf16[6144,4]{0,1:T(4,128)(2,1)S(1)}, bf16[6144,4]{0,1:T(4,128)(2,1)}, u32[]{:S(2)}) copy-start(bf16[6144,4]{0,1:T(4,128)(2,1)} %param.17) | copy-start | bytes 147460
  109.7 14.2 %copy-start.2 = (bf16[4,6144]{1,0:T(4,128)(2,1)}, bf16[4,6144]{1,0:T(4,128)(2,1)S(1)}, u32[]{:S(2)}) copy-start(bf16[4,6144]{1,0:T(4,128)(2,1)S(1)} %multiply_convert_fusion) | copy-start | bytes 147460
  184.1 8.7 %all-to-all-start.1 = ((f32[4,2,6144]{2,1,0:T(2,128)}), f32[4,2,6144]{2,1,0:T(2,128)S(1)}, u32[]{:S(2)}, u32[]{:S(2)}) async-start(f32[4,2,6144]{2,1,0:T(2,128)} %reduce_sum.89), calls=%async_computation.1 | async-start | bytes 393216 | tf_op jit(solution)/shard_map/all_to_all | solution.py:101
Sparse Core Ops, SparseCore 0:
  136.6 44.6 all-gather.5
